TPU v7x, 256 devices: a whole 4x4x8 slice. The times are simulated.
256 devices in a mesh: seq: 32 (over y, z_hi, core), head: 8 (over z_lo, x).
Axes of the slice: x: 4, y: 4, z: 8 (z_hi: 4, z_lo: 2; z = z_hi * 2 + z_lo), core: 2. Of those that a mesh axis runs over, the one named last changes fastest.
Arguments:
- xin: bfloat16 [16384, 8192], P('seq', 'head'), may hold values from -6 to 6
- gate_z: bfloat16 [16384, 8192], P('seq', 'head'), may hold values from -6 to 6
- b_proj: bfloat16 [16384, 8, 256], P('seq', 'head'), may hold values from -0.375 to 0.375
- c_proj: bfloat16 [16384, 8, 256], P('seq', 'head'), may hold values from -0.375 to 0.375
- log_retain: float32 [16384, 128], P('seq', 'head'), may hold values from -2 to 0, as said below
- skip_d: float32 [128], P('head'), may hold values from 0.5 to 2
- norm_gain: float32 [8192], P('head'), may hold values from 0.5 to 1.5
- w_out: bfloat16 [8192, 4096], P('head', 'seq'), may hold values from -0.0625 to 0.0625
- residual: bfloat16 [16384, 4096], P(('seq', 'head')), may hold values from -24 to 24
- refusal: float32 [4096], replicated, may hold values from -6 to 6
- stream_gain: float32 [4096], replicated, may hold values from 0.5 to 1.5
- w_in: bfloat16 [4096, 8192], P('seq', 'head'), may hold values from -0.09375 to 0.09375
Outputs:
- stream: bfloat16 [16384, 4096], P(('seq', 'head'))
- next_x: bfloat16 [16384, 8192], P('seq', 'head')
Inputs may be any that keep to these rules, and one draw needn't show every extreme that they name: `log_retain`: every entry is negative.
All inputs are finite; a program needn't handle non-finite values.
Results may differ from a plain program's by a relative error of at most 0.02.
Values may be sent and summed in bfloat16 or wider, within the bound.
No kernel may reach another device: no remote copies, remote signals or barrier semaphores. Data moves between devices by JAX's collectives and lax.ppermute only.
A program may use at most 192 MiB of HBM per device.

v0:
```python
import jax
import jax.numpy as jnp
from jax import lax
from jax.sharding import PartitionSpec as P

SPAN = 256


def shift_scan(decay, state, axis):
    devices = lax.axis_size(axis)

    def shifted(parts, distance):
        pairs = [(i, i + distance) for i in range(devices - distance)]
        a, s = parts
        return (
            lax.ppermute(a, axis, pairs),
            lax.ppermute(s.astype(jnp.bfloat16), axis, pairs).astype(jnp.float32),
        )

    acc = shifted((decay, state), 1)
    distance = 1
    while distance < devices:
        acc = carry_combine(shifted(acc, distance), acc)
        distance *= 2
    return acc


def carry_combine(earlier, later):
    decay_early, state_early = earlier
    decay_later, state_later = later
    return (
        decay_early + decay_later,
        jnp.exp(decay_later).reshape((-1,) + (1,) * (state_later.ndim - 1)) * state_early
        + state_later,
    )


def body(
    xin,
    gate_z,
    b_proj,
    c_proj,
    log_retain,
    skip_d,
    norm_gain,
    w_out,
    residual,
    refusal,
    stream_gain,
    w_in,
):
    seq_rows, channels = xin.shape
    head_count = log_retain.shape[1]
    head_width = channels // head_count
    group_count = b_proj.shape[1]
    state_width = b_proj.shape[2]
    per_group = head_count // group_count
    block_count = seq_rows // SPAN
    inputs = xin.reshape(block_count, SPAN, head_count, head_width)
    b_grouped = b_proj.reshape(block_count, SPAN, group_count, state_width)
    c_grouped = c_proj.reshape(block_count, SPAN, group_count, state_width)
    scores = jnp.einsum("klgn,ksgn->kgls", c_grouped, b_grouped, preferred_element_type=jnp.float32)
    scores = jnp.repeat(scores, per_group, axis=1)
    cum = jnp.cumsum(log_retain.reshape(block_count, SPAN, head_count), axis=1)
    cum_heads = jnp.transpose(cum, (0, 2, 1))
    later_pos = lax.broadcasted_iota(jnp.int32, (SPAN, SPAN), 0)
    earlier_pos = lax.broadcasted_iota(jnp.int32, (SPAN, SPAN), 1)
    causal = later_pos >= earlier_pos
    gap = cum_heads[:, :, :, None] - cum_heads[:, :, None, :]
    mixing = (jnp.where(causal, jnp.exp(jnp.where(causal, gap, 0.0)), 0.0) * scores).astype(
        jnp.bfloat16
    )
    intra = jnp.einsum("khls,kshp->klhp", mixing, inputs, preferred_element_type=jnp.float32)
    tail_decay = jnp.exp(cum_heads[:, :, -1:] - cum_heads)
    b_heads = jnp.repeat(b_grouped, per_group, axis=2)
    weighted_b = (
        b_heads.astype(jnp.float32) * jnp.transpose(tail_decay, (0, 2, 1))[..., None]
    ).astype(jnp.bfloat16)
    block_state = jnp.einsum(
        "klhn,klhp->khnp", weighted_b, inputs, preferred_element_type=jnp.float32
    )
    block_decay = cum_heads[:, :, -1]
    device_state = jnp.zeros((head_count, state_width, head_width), jnp.float32)
    starts_list = []
    for block in range(block_count):
        starts_list.append(device_state)
        device_state = (
            jnp.exp(block_decay[block])[:, None, None] * device_state + block_state[block]
        )
    local_starts = jnp.stack(starts_list)
    device_decay = jnp.sum(block_decay, axis=0)
    total_decay, incoming = shift_scan(
        device_decay, device_state.reshape(head_count, state_width * head_width), "seq"
    )
    incoming = incoming.reshape(head_count, state_width, head_width)
    before_block = jnp.cumsum(block_decay, axis=0) - block_decay
    starts = local_starts + jnp.exp(before_block)[:, :, None, None] * incoming[None]
    c_heads = jnp.repeat(c_grouped, per_group, axis=2).astype(jnp.float32)
    carried = jnp.einsum("klhn,khnp->klhp", c_heads, starts, precision=lax.Precision.HIGHEST)
    carried = carried * jnp.exp(cum)[..., None]
    mixed = intra + carried + skip_d[None, None, :, None] * inputs.astype(jnp.float32)
    gated = mixed * jax.nn.silu(
        gate_z.reshape(block_count, SPAN, head_count, head_width).astype(jnp.float32)
    )
    grouped = gated.reshape(seq_rows, group_count, per_group * head_width)
    grouped = grouped * lax.rsqrt(jnp.mean(grouped * grouped, axis=-1, keepdims=True) + 1e-05)
    ssd_out = (grouped.reshape(seq_rows, channels) * norm_gain[None, :]).astype(jnp.bfloat16)
    w_in_all = lax.all_gather(w_in, "seq", axis=0, tiled=True)
    ssd_out, w_in_all = lax.optimization_barrier((ssd_out, w_in_all))
    own_rows = residual.shape[0]
    mine = lax.axis_index("head")
    head_devices = seq_rows // own_rows
    in_block = lax.broadcasted_iota(jnp.int32, (head_devices, 1, 1), 0) == mine
    residual_rows = jnp.where(in_block, residual.astype(jnp.float32)[None], 0.0).reshape(
        seq_rows, residual.shape[1]
    )
    partial_sum = jnp.dot(
        ssd_out,
        lax.all_gather(w_out, "seq", axis=1, tiled=True),
        preferred_element_type=jnp.float32,
    )
    with_residual = (partial_sum + residual_rows).astype(jnp.bfloat16)
    hidden = lax.psum(with_residual, "head").astype(jnp.float32)
    unit = refusal / jnp.sqrt(jnp.sum(refusal * refusal) + 1e-06)
    coef = jnp.dot(hidden, unit, precision=lax.Precision.HIGH)
    stream_all = (hidden - coef[:, None] * unit[None, :]).astype(jnp.bfloat16)
    stream_float = stream_all.astype(jnp.float32)
    all_rows = (
        stream_float
        * lax.rsqrt(jnp.mean(stream_float * stream_float, axis=-1, keepdims=True) + 1e-05)
        * stream_gain[None, :]
    ).astype(jnp.bfloat16)
    stream = lax.dynamic_slice_in_dim(stream_all, mine * own_rows, own_rows)
    next_float = jnp.dot(all_rows, w_in_all, preferred_element_type=jnp.float32)
    return (stream, next_float.astype(jnp.bfloat16))


def solution(mesh):
    in_specs = (
        P("seq", "head"),
        P("seq", "head"),
        P("seq", "head", None),
        P("seq", "head", None),
        P("seq", "head"),
        P("head"),
        P("head"),
        P("head", "seq"),
        P(("seq", "head"), None),
        P(),
        P(),
        P("seq", "head"),
    )
    out_specs = (P(("seq", "head"), None), P("seq", "head"))
    return jax.shard_map(body, mesh=mesh, in_specs=in_specs, out_specs=out_specs, check_vma=False)
```

profile of v0, /device:TPU:1, one launch (start us, length us, event | category | flops | bytes accessed | tf_op | source)
XLA Modules:
  0.0 363.6 jit_solution(14837152535283461224)
XLA Ops:
  7.2 0.7 all-gather.3.cloned.1.call-update
  8.0 0.8 copy_bitcast_fusion.1
  8.7 1.1 reduce-window.6
  10.1 3.0 reshape.187
  13.0 1.7 copy.36
  14.7 1.2 convert_element_type.79
  16.4 0.7 exponential_bitcast_fusion
  17.1 1.6 fusion.6
  18.7 1.6 fusion.43
  21.6 1.8 copy.38
  23.4 1.7 squeeze.4
  25.1 1.4 add_convert_fusion
  26.6 6.3 %collective-permute-start.5 = (bf16[16,16384]{1,0:T(8,128)(2,1)S(1)}, bf16[16,16384]{1,0:T(8,128)(2,1)S(1)}, u32[]{:S(2)}, u32[]{:S(2)}) collective-permute-start(bf16[16,16384]{1,0:T(8,128)(2,1)S(1)} %add_convert_fusion), channel_id=1, source_target_pairs={{0,8},{8,16},{16,24},{24,32},{32,40},{40,48},{48,56},{56,64},{64,7... | collective-permute-start | bytes 1572872 | tf_op jit(solution)/shard_map/ppermute | solution.py:17
  32.9 15.5 %collective-permute-done.5 = bf16[16,16384]{1,0:T(8,128)(2,1)S(1)} collective-permute-done((bf16[16,16384]{1,0:T(8,128)(2,1)S(1)}, bf16[16,16384]{1,0:T(8,128)(2,1)S(1)}, u32[]{:S(2)}, u32[]{:S(2)}) %collective-permute-start.5) | collective-permute-done | bytes 524320 | tf_op jit(solution)/shard_map/ppermute | solution.py:17
  48.4 6.1 %collective-permute-start.6 = (bf16[16,16384]{1,0:T(8,128)(2,1)S(1)}, bf16[16,16384]{1,0:T(8,128)(2,1)S(1)}, u32[]{:S(2)}, u32[]{:S(2)}) collective-permute-start(bf16[16,16384]{1,0:T(8,128)(2,1)S(1)} %collective-permute-done.5), channel_id=1, source_target_pairs={{0,8},{8,16},{16,24},{24,32},{32,40},{40,48},{48,56},{56,64},{64,7... | collective-permute-start | bytes 1572872 | tf_op jit(solution)/shard_map/ppermute | solution.py:17
  54.5 2.5 collective-permute-start
  57.1 20.6 %collective-permute-done = f32[16]{0:T(128)S(1)} collective-permute-done((f32[16]{0:T(128)S(1)}, f32[16]{0:T(128)S(1)}, u32[]{:S(2)}, u32[]{:S(2)}) %collective-permute-start) | collective-permute-done | bytes 96 | tf_op jit(solution)/shard_map/ppermute | solution.py:16
  77.7 5.7 %collective-permute-start.1 = (f32[16]{0:T(128)S(1)}, f32[16]{0:T(128)S(1)}, u32[]{:S(2)}, u32[]{:S(2)}) collective-permute-start(f32[16]{0:T(128)S(1)} %collective-permute-done), channel_id=1, source_target_pairs={{0,8},{8,16},{16,24},{24,32},{32,40},{40,48},{48,56},{56,64},{64,7... | collective-permute-start | bytes 200 | tf_op jit(solution)/shard_map/ppermute | solution.py:16
  83.4 0.7 collective-permute-done.1
  84.3 23.8 %collective-permute-start.7 = (bf16[16,16384]{1,0:T(8,128)(2,1)S(1)}, bf16[16,16384]{1,0:T(8,128)(2,1)S(1)}, u32[]{:S(2)}, u32[]{:S(2)}) collective-permute-start(bf16[16,16384]{1,0:T(8,128)(2,1)S(1)} %fusion.31), channel_id=1, source_target_pairs={{0,16},{8,24},{16,32},{24,40},{32,48},{40,56},{48,64},{56,72},{64,... | collective-permute-start | bytes 1572872 | tf_op jit(solution)/shard_map/ppermute | solution.py:17
  108.2 13.9 %collective-permute-done.7 = bf16[16,16384]{1,0:T(8,128)(2,1)S(1)} collective-permute-done((bf16[16,16384]{1,0:T(8,128)(2,1)S(1)}, bf16[16,16384]{1,0:T(8,128)(2,1)S(1)}, u32[]{:S(2)}, u32[]{:S(2)}) %collective-permute-start.7) | collective-permute-done | bytes 524320 | tf_op jit(solution)/shard_map/ppermute | solution.py:17
  122.5 10.4 %collective-permute-start.8 = (bf16[16,16384]{1,0:T(8,128)(2,1)S(1)}, bf16[16,16384]{1,0:T(8,128)(2,1)S(1)}, u32[]{:S(2)}, u32[]{:S(2)}) collective-permute-start(bf16[16,16384]{1,0:T(8,128)(2,1)S(1)} %fusion.39), channel_id=1, source_target_pairs={{0,32},{8,40},{16,48},{24,56},{32,64},{40,72},{48,80},{56,88},{64,... | collective-permute-start | bytes 1572872 | tf_op jit(solution)/shard_map/ppermute | solution.py:17
  133.0 2.1 collective-permute-start.2
  135.0 24.5 %collective-permute-done.2 = f32[16]{0:T(128)S(1)} collective-permute-done((f32[16]{0:T(128)S(1)}, f32[16]{0:T(128)S(1)}, u32[]{:S(2)}, u32[]{:S(2)}) %collective-permute-start.2) | collective-permute-done | bytes 96 | tf_op jit(solution)/shard_map/ppermute | solution.py:16
  160.0 1.5 collective-permute-start.9
  161.5 8.3 %collective-permute-start.3 = (f32[16]{0:T(128)S(1)}, f32[16]{0:T(128)S(1)}, u32[]{:S(2)}, u32[]{:S(2)}) collective-permute-start(f32[16]{0:T(128)S(1)} %get-tuple-element.15), channel_id=1, source_target_pairs={{0,32},{8,40},{16,48},{24,56},{32,64},{40,72},{48,80},{56,88},{64,... | collective-permute-start | bytes 200 | tf_op jit(solution)/shard_map/ppermute | solution.py:16
  169.8 0.7 collective-permute-done.3
  170.5 1.3 fusion.38
  171.9 15.1 %collective-permute-start.10 = (bf16[16,16384]{1,0:T(8,128)(2,1)}, bf16[16,16384]{1,0:T(8,128)(2,1)}, u32[]{:S(2)}, u32[]{:S(2)}) collective-permute-start(bf16[16,16384]{1,0:T(8,128)(2,1)} %fusion.38), channel_id=1, source_target_pairs={{0,128},{8,136},{16,144},{24,152},{32,160},{40,168},{48,176},{56,1... | collective-permute-start | bytes 1572872 | tf_op jit(solution)/shard_map/ppermute | solution.py:17
  186.9 4.1 %reshape.188 = f32[2,256,16,64]{3,2,1,0:T(8,128)} reshape(bf16[512,1024]{1,0:T(8,128)(2,1)} %param.13) | data formatting | bytes 3145728 | tf_op jit(solution)/shard_map/convert_element_type | solution.py:103
  191.0 4.6 %copy.44 = f32[2,256,16,64]{1,3,2,0:T(8,128)} copy(f32[2,256,16,64]{3,2,1,0:T(8,128)} %reshape.188) | data formatting | bytes 4194304 | tf_op jit(solution)/shard_map/convert_element_type | solution.py:103
  195.8 1.1 fusion.44
  196.9 1.5 collective-permute-start.4
  198.3 2.1 convert_element_type.96
  200.9 2.7 multiply_add_fusion
  203.6 2.1 mul.195
  206.3 5.3 %fusion.21 = f32[2,16,64,256]{3,2,1,0:T(8,128)S(1)} fusion(bf16[2,256,256]{2,1,0:T(8,128)(2,1)S(1)} %bitcast.66, f32[1,16,256,64]{2,3,1,0:T(8,128)} %get-tuple-element.19, f32[16,256,64]{1,2,0:T(8,128)S(1)} %copy.40, f32[2,16]{1,0:T(2,128)S(1)} %subtract_exponential_fusion), kind=kOutput, calls=%fused_computation.29 | convolution fusion | flops 1611661312 | bytes 4456576 | tf_op jit(solution)/shard_map/klhn,khnp->klhp/dot_general | solution.py:99
  211.7 3.1 multiply_reduce_fusion
  214.8 1.6 copy.45
  216.9 8.2 %all-gather.5.cloned.1.call-done = bf16[1024,4096]{1,0:T(8,128)(2,1)} async-done(((bf16[1024,128]{1,0:T(8,128)(2,1)}), bf16[1024,4096]{1,0:T(8,128)(2,1)}) %all-gather.5.cloned.1.call-update) | async-done | bytes 8388624 | tf_op jit(solution)/shard_map/all_gather | solution.py:119
  225.2 9.7 %fusion.4 = bf16[512,4096]{1,0:T(8,128)(2,1)} fusion(bf16[512,1024]{0,1:T(8,128)(2,1)S(1)} %multiply_convert_fusion.4, bf16[1024,4096]{1,0:T(8,128)(2,1)} %all-gather.5.cloned.1.call-done, f32[64,4096]{1,0:T(8,128)S(1)} %copy-done.6, pred[512]{0:T(512)(128)(4,1)S(1)} %broadcast_in_dim.63), kind=kOutput, calls=%fused_computation.7 | convolution fusion | flops 4301258752 | bytes 14680576 | tf_op jit(solution)/shard_map/dot_general | solution.py:117
  234.9 0.7 copy-done.9
  236.9 106.3 %all-reduce.3.cloned.1.call-done = bf16[512,4096]{1,0:T(8,128)(2,1)} async-done(((bf16[512,4096]{1,0:T(8,128)(2,1)}), bf16[512,4096]{1,0:T(8,128)(2,1)}) %all-reduce.3.cloned.1.call-update) | async-done | bytes 4194320 | tf_op jit(solution)/shard_map/psum | solution.py:123
  343.3 4.6 %fusion.45 = f32[1,512]{1,0:T(1,128)S(1)} fusion(bf16[512,4096]{1,0:T(8,128)(2,1)} %all-reduce.3.cloned.1.call-done, f32[4096,1]{0,1:T(1,128)S(1)} %bitcast.71), kind=kOutput, calls=%fused_computation.78 | convolution fusion | flops 12582912 | bytes 4212736 | tf_op jit(solution)/shard_map/dot_general | solution.py:125
  347.9 1.9 fusion
  349.8 0.8 constant_dynamic-slice_fusion
  350.7 0.8 copy-done.12
  351.5 5.6 %fusion.26 = bf16[512,1024]{1,0:T(8,128)(2,1)} fusion(bf16[4096,1024]{1,0:T(8,128)(2,1)S(1)} %copy-done.12, bf16[512,4096]{1,0:T(8,128)(2,1)S(1)} %get-tuple-element.11, f32[4096]{0:T(1024)S(1)} %copy-done.13, f32[512]{0:T(512)S(1)} %add_rsqrt_fusion), kind=kOutput, calls=%fused_computation.34 | convolution fusion | flops 4303880192 | bytes 13649920 | tf_op jit(solution)/shard_map/dot_general | solution.py:134
  (68 shorter events, 5.6 us)
Async XLA Ops:
  7.2 188.6 %copy-start = (bf16[512,1,256]{2,0,1:T(8,128)(2,1)S(1)}, bf16[512,1,256]{2,0,1:T(8,128)(2,1)}, u32[]{:S(2)}) copy-start(bf16[512,1,256]{2,0,1:T(8,128)(2,1)} %param.15) | copy-start | bytes 786436
  7.2 209.7 %all-gather.3.cloned.1.call-start = ((), (), s32[]{:S(2)}) async-start(), calls=%async_computation | async-start | bytes 8650752 | tf_op jit(solution)/shard_map/all_gather | solution.py:108
  7.9 217.2 %all-gather.5.cloned.1.call-start = ((), (), s32[]{:S(2)}) async-start(), calls=%async_computation.1 | async-start | bytes 8650752 | tf_op jit(solution)/shard_map/all_gather | solution.py:119
  14.7 5.6 %copy-start.4 = (bf16[2,256,16,64]{1,3,2,0:T(8,128)(2,1)}, bf16[2,256,16,64]{1,3,2,0:T(8,128)(2,1)S(1)}, u32[]{:S(2)}) copy-start(bf16[2,256,16,64]{1,3,2,0:T(8,128)(2,1)S(1)} %copy.36) | copy-start | bytes 3145732
  26.6 21.8 %collective-permute-start.5 = (bf16[16,16384]{1,0:T(8,128)(2,1)S(1)}, bf16[16,16384]{1,0:T(8,128)(2,1)S(1)}, u32[]{:S(2)}, u32[]{:S(2)}) collective-permute-start(bf16[16,16384]{1,0:T(8,128)(2,1)S(1)} %add_convert_fusion), channel_id=1, source_target_pairs={{0,8},{8,16},{16,24},{24,32},{32,40},{40,48},{48,56},{56,64},{64,7... | collective-permute-start | bytes 1572872 | tf_op jit(solution)/shard_map/ppermute | solution.py:17
  48.4 35.7 %collective-permute-start.6 = (bf16[16,16384]{1,0:T(8,128)(2,1)S(1)}, bf16[16,16384]{1,0:T(8,128)(2,1)S(1)}, u32[]{:S(2)}, u32[]{:S(2)}) collective-permute-start(bf16[16,16384]{1,0:T(8,128)(2,1)S(1)} %collective-permute-done.5), channel_id=1, source_target_pairs={{0,8},{8,16},{16,24},{24,32},{32,40},{40,48},{48,56},{56,64},{64,7... | collective-permute-start | bytes 1572872 | tf_op jit(solution)/shard_map/ppermute | solution.py:17
  54.5 23.2 %collective-permute-start = (f32[16]{0:T(128)S(1)}, f32[16]{0:T(128)S(1)}, u32[]{:S(2)}, u32[]{:S(2)}) collective-permute-start(f32[16]{0:T(128)S(1)} %get-tuple-element.6), channel_id=1, source_target_pairs={{0,8},{8,16},{16,24},{24,32},{32,40},{40,48},{48,56},{56,64},{64,7... | collective-permute-start | bytes 200 | tf_op jit(solution)/shard_map/ppermute | solution.py:16
  77.7 6.4 %collective-permute-start.1 = (f32[16]{0:T(128)S(1)}, f32[16]{0:T(128)S(1)}, u32[]{:S(2)}, u32[]{:S(2)}) collective-permute-start(f32[16]{0:T(128)S(1)} %collective-permute-done), channel_id=1, source_target_pairs={{0,8},{8,16},{16,24},{24,32},{32,40},{40,48},{48,56},{56,64},{64,7... | collective-permute-start | bytes 200 | tf_op jit(solution)/shard_map/ppermute | solution.py:16
  84.3 37.8 %collective-permute-start.7 = (bf16[16,16384]{1,0:T(8,128)(2,1)S(1)}, bf16[16,16384]{1,0:T(8,128)(2,1)S(1)}, u32[]{:S(2)}, u32[]{:S(2)}) collective-permute-start(bf16[16,16384]{1,0:T(8,128)(2,1)S(1)} %fusion.31), channel_id=1, source_target_pairs={{0,16},{8,24},{16,32},{24,40},{32,48},{40,56},{48,64},{56,72},{64,... | collective-permute-start | bytes 1572872 | tf_op jit(solution)/shard_map/ppermute | solution.py:17
  108.2 235.1 %all-reduce.3.cloned.1.call-start = ((), (), s32[]{:S(2)}) async-start(), calls=%async_computation.2 | async-start | bytes 8388608 | tf_op jit(solution)/shard_map/psum | solution.py:123
  122.5 37.0 %collective-permute-start.8 = (bf16[16,16384]{1,0:T(8,128)(2,1)S(1)}, bf16[16,16384]{1,0:T(8,128)(2,1)S(1)}, u32[]{:S(2)}, u32[]{:S(2)}) collective-permute-start(bf16[16,16384]{1,0:T(8,128)(2,1)S(1)} %fusion.39), channel_id=1, source_target_pairs={{0,32},{8,40},{16,48},{24,56},{32,64},{40,72},{48,80},{56,88},{64,... | collective-permute-start | bytes 1572872 | tf_op jit(solution)/shard_map/ppermute | solution.py:17
  133.0 26.5 %collective-permute-start.2 = (f32[16]{0:T(128)S(1)}, f32[16]{0:T(128)S(1)}, u32[]{:S(2)}, u32[]{:S(2)}) collective-permute-start(f32[16]{0:T(128)S(1)} %get-tuple-element.17), channel_id=1, source_target_pairs={{0,16},{8,24},{16,32},{24,40},{32,48},{40,56},{48,64},{56,72},{64,... | collective-permute-start | bytes 200 | tf_op jit(solution)/shard_map/ppermute | solution.py:16
  160.0 10.6 %collective-permute-start.9 = (bf16[16,16384]{1,0:T(8,128)(2,1)S(1)}, bf16[16,16384]{1,0:T(8,128)(2,1)S(1)}, u32[]{:S(2)}, u32[]{:S(2)}) collective-permute-start(bf16[16,16384]{1,0:T(8,128)(2,1)S(1)} %fusion.32), channel_id=1, source_target_pairs={{0,64},{8,72},{16,80},{24,88},{32,96},{40,104},{48,112},{56,120},{... | collective-permute-start | bytes 1572872 | tf_op jit(solution)/shard_map/ppermute | solution.py:17
  161.5 9.0 %collective-permute-start.3 = (f32[16]{0:T(128)S(1)}, f32[16]{0:T(128)S(1)}, u32[]{:S(2)}, u32[]{:S(2)}) collective-permute-start(f32[16]{0:T(128)S(1)} %get-tuple-element.15), channel_id=1, source_target_pairs={{0,32},{8,40},{16,48},{24,56},{32,64},{40,72},{48,80},{56,88},{64,... | collective-permute-start | bytes 200 | tf_op jit(solution)/shard_map/ppermute | solution.py:16
  171.9 29.1 %collective-permute-start.10 = (bf16[16,16384]{1,0:T(8,128)(2,1)}, bf16[16,16384]{1,0:T(8,128)(2,1)}, u32[]{:S(2)}, u32[]{:S(2)}) collective-permute-start(bf16[16,16384]{1,0:T(8,128)(2,1)} %fusion.38), channel_id=1, source_target_pairs={{0,128},{8,136},{16,144},{24,152},{32,160},{40,168},{48,176},{56,1... | collective-permute-start | bytes 1572872 | tf_op jit(solution)/shard_map/ppermute | solution.py:17
  191.0 4.8 %copy-start.7 = (bf16[512,1,256]{2,0,1:T(8,128)(2,1)S(1)}, bf16[512,1,256]{2,0,1:T(8,128)(2,1)}, u32[]{:S(2)}) copy-start(bf16[512,1,256]{2,0,1:T(8,128)(2,1)} %param.14) | copy-start | bytes 786436
  196.9 4.1 %collective-permute-start.4 = (f32[16]{0:T(128)S(1)}, f32[16]{0:T(128)S(1)}, u32[]{:S(2)}, u32[]{:S(2)}) collective-permute-start(f32[16]{0:T(128)S(1)} %get-tuple-element.13), channel_id=1, source_target_pairs={{0,64},{8,72},{16,80},{24,88},{32,96},{40,104},{48,112},{56,120},{... | collective-permute-start | bytes 200 | tf_op jit(solution)/shard_map/ppermute | solution.py:16
  205.7 6.0 %copy-start.10 = (f32[2,256,16]{1,2,0:T(8,128)S(1)}, f32[2,256,16]{1,2,0:T(8,128)}, u32[]{:S(2)}) copy-start(f32[2,256,16]{1,2,0:T(8,128)} %get-tuple-element.21) | copy-start | bytes 98308
  205.7 6.0 %copy-start.14 = (f32[16]{0:T(128)S(1)}, f32[16]{0:T(128)}, u32[]{:S(2)}) copy-start(f32[16]{0:T(128)} %param.17) | copy-start | bytes 196
  206.3 5.4 %copy-start.3 = (f32[2,256,16,64]{1,3,2,0:T(8,128)S(1)}, f32[2,256,16,64]{1,3,2,0:T(8,128)}, u32[]{:S(2)}) copy-start(f32[2,256,16,64]{1,3,2,0:T(8,128)} %copy.44) | copy-start | bytes 6291460
  206.3 5.4 %copy-start.5 = (bf16[2,256,16,64]{1,3,2,0:T(8,128)(2,1)S(1)}, bf16[2,256,16,64]{1,3,2,0:T(8,128)(2,1)}, u32[]{:S(2)}) copy-start(bf16[2,256,16,64]{1,3,2,0:T(8,128)(2,1)} %copy-done.4) | copy-start | bytes 3145732
  206.3 5.4 %copy-start.8 = (f32[2,256,256]{2,1,0:T(8,128)S(1)}, f32[2,256,256]{2,1,0:T(8,128)}, u32[]{:S(2)}) copy-start(f32[2,256,256]{2,1,0:T(8,128)} %fusion.44) | copy-start | bytes 1572868
  214.8 1.9 copy-start.11
  216.4 8.8 %copy-start.6 = (f32[64,4096]{1,0:T(8,128)S(1)}, f32[64,4096]{1,0:T(8,128)}, u32[]{:S(2)}) copy-start(f32[64,4096]{1,0:T(8,128)} %convert_element_type.96) | copy-start | bytes 3145732
  234.9 0.7 copy-start.9
  343.3 4.6 %copy-start.2 = (bf16[512,4096]{1,0:T(8,128)(2,1)S(1)}, bf16[512,4096]{1,0:T(8,128)(2,1)}, u32[]{:S(2)}) copy-start(bf16[512,4096]{1,0:T(8,128)(2,1)} %all-reduce.3.cloned.1.call-done) | copy-start | bytes 12582916
  347.9 3.6 copy-start.12
  347.9 3.6 copy-start.13
  351.5 5.6 %copy-start.1 = (bf16[512,1,256]{2,0,1:T(8,128)(2,1)S(1)}, bf16[512,1,256]{2,0,1:T(8,128)(2,1)}, u32[]{:S(2)}) copy-start(bf16[512,1,256]{2,0,1:T(8,128)(2,1)} %param.15) | copy-start | bytes 786436
Sparse Core Ops, SparseCore 0:
  10.6 109.2 all-gather.2
  122.3 102.8 all-gather.4
  235.1 108.1 all-reduce.2
where the time goes:
time: 364 us
  waiting for transfers between devices  192 us (53%)
  starting transfers between devices  83.4 us (23%)
  matrix products  31 us (9%)
  local copies, waits for them, and re-layouts  26.1 us (7%)
  other arithmetic  16.6 us (5%)
  between operations  14.8 us (4%)
    psum x1, waiting for transfers between devices, body(): hidden = lax.psum(with_residual, 'head').astype(jnp.float32)  106 us
    ppermute x6, starting transfers between devices, shifted(): lax.ppermute(s.astype(jnp.bfloat16), axis, pairs).astype(jnp.float32)  63.3 us
    ppermute x5, waiting for transfers between devices, shifted(): lax.ppermute(a, axis, pairs)  47 us
    ppermute x6, waiting for transfers between devices, shifted(): lax.ppermute(s.astype(jnp.bfloat16), axis, pairs).astype(jnp.float32)  29.4 us
    ppermute x5, starting transfers between devices, shifted(): lax.ppermute(a, axis, pairs)  20 us
    dot_general x1, matrix products, body(): jnp.dot(ssd_out, lax.all_gather(w_out, 'seq', axis=1, tiled=True), prefer...  9.75 us
    convert_element_type x2, local copies, waits for them, and re-layouts, body(): gate_z.reshape(block_count, SPAN, head_count, head_width)  8.7 us
    all_gather x1, waiting for transfers between devices, body(): lax.all_gather(w_out, 'seq', axis=1, tiled=True)  8.23 us
  transfers between devices with their start and end apart: 14, of which 9 were waited for; matrix products, arithmetic and copies ran while one was open for 14% of the time, Pallas kernels for 0%

commit v1 on v0

--- a/solution.py
+++ b/solution.py
@@ -120,7 +120,7 @@
         preferred_element_type=jnp.float32,
     )
     with_residual = (partial_sum + residual_rows).astype(jnp.bfloat16)
-    hidden = lax.psum(with_residual, "head").astype(jnp.float32)
+    hidden = jnp.sum(lax.all_gather(with_residual, axis_name="head"), axis=0).astype(jnp.float32)
     unit = refusal / jnp.sqrt(jnp.sum(refusal * refusal) + 1e-06)
     coef = jnp.dot(hidden, unit, precision=lax.Precision.HIGH)
     stream_all = (hidden - coef[:, None] * unit[None, :]).astype(jnp.bfloat16)

time: 364 us -> 602 us (1.65)
  waiting for transfers between devices: 192 us -> 385 us
  starting transfers between devices: 83.4 us -> 114 us
  other arithmetic: 16.6 us -> 29.8 us
    all_gather x0 -> x1, waiting for transfers between devices: none -> 326 us  [body(): lax.all_gather(with_residual, axis_name='head')]
    psum x1 -> x0, waiting for transfers between devices: 106 us -> none  [body(): hidden = lax.psum(with_residual, 'head').astype(jnp.float32)]
    ppermute x6, starting transfers between devices: 63.3 us -> 99.8 us  [shifted(): lax.ppermute(s.astype(jnp.bfloat16), axis, pairs).astype(jnp.float32)]
    ppermute x5, waiting for transfers between devices: 47 us -> 21.7 us  [shifted(): lax.ppermute(a, axis, pairs)]
    reduce_sum x0 -> x1, other arithmetic: none -> 14 us  [body(): jnp.sum(lax.all_gather(with_residual, axis_name='head'), axis=0)]
  transfers between devices with their start and end apart: 14 -> 14, of which waited for: 9 -> 9; matrix products, arithmetic and copies ran while one was open for 14% -> 8% of each run, Pallas kernels for 0% -> 0%
where the time goes in v1:
time: 602 us; the launch traced here: 601 us
  waiting for transfers between devices  385 us (64%)
  starting transfers between devices  114 us (19%)
  matrix products  33.6 us (6%)
  other arithmetic  29.8 us (5%)
  local copies, waits for them, and re-layouts  24 us (4%)
  between operations  14.8 us (2%)
    all_gather x1, waiting for transfers between devices, body(): lax.all_gather(with_residual, axis_name='head')  326 us
    ppermute x6, starting transfers between devices, shifted(): lax.ppermute(s.astype(jnp.bfloat16), axis, pairs).astype(jnp.float32)  99.8 us
    ppermute x6, waiting for transfers between devices, shifted(): lax.ppermute(s.astype(jnp.bfloat16), axis, pairs).astype(jnp.float32)  25.1 us
    ppermute x5, waiting for transfers between devices, shifted(): lax.ppermute(a, axis, pairs)  21.7 us
    ppermute x5, starting transfers between devices, shifted(): lax.ppermute(a, axis, pairs)  14.3 us
    reduce_sum x1, other arithmetic, body(): jnp.sum(lax.all_gather(with_residual, axis_name='head'), axis=0)  14 us
  transfers between devices with their start and end apart: 14, of which 9 were waited for; matrix products, arithmetic and copies ran while one was open for 8% of the time, Pallas kernels for 0%

profile of v1, /device:TPU:1, one launch (start us, length us, event | category | flops | bytes accessed | tf_op | source)
XLA Modules:
  0.0 601.5 jit_solution(6095658802147858071)
XLA Ops:
  8.0 0.8 copy_bitcast_fusion.1
  8.7 1.1 reduce-window.6
  10.1 3.0 reshape.188
  13.0 1.7 copy.36
  14.7 1.2 convert_element_type.81
  16.4 0.7 exponential_bitcast_fusion
  17.1 1.6 fusion.6
  18.7 1.6 fusion.43
  21.6 1.8 copy.38
  23.4 1.6 squeeze.4
  25.0 1.4 add_convert_fusion
  26.4 6.3 %collective-permute-start.5 = (bf16[16,16384]{1,0:T(8,128)(2,1)S(1)}, bf16[16,16384]{1,0:T(8,128)(2,1)S(1)}, u32[]{:S(2)}, u32[]{:S(2)}) collective-permute-start(bf16[16,16384]{1,0:T(8,128)(2,1)S(1)} %add_convert_fusion), channel_id=1, source_target_pairs={{0,8},{8,16},{16,24},{24,32},{32,40},{40,48},{48,56},{56,64},{64,7... | collective-permute-start | bytes 1572872 | tf_op jit(solution)/shard_map/ppermute | solution.py:17
  32.8 15.2 %collective-permute-done.5 = bf16[16,16384]{1,0:T(8,128)(2,1)S(1)} collective-permute-done((bf16[16,16384]{1,0:T(8,128)(2,1)S(1)}, bf16[16,16384]{1,0:T(8,128)(2,1)S(1)}, u32[]{:S(2)}, u32[]{:S(2)}) %collective-permute-start.5) | collective-permute-done | bytes 524320 | tf_op jit(solution)/shard_map/ppermute | solution.py:17
  47.9 5.3 collective-permute-start.6
  53.2 3.9 collective-permute-start
  57.1 8.2 %collective-permute-done = f32[16]{0:T(128)S(1)} collective-permute-done((f32[16]{0:T(128)S(1)}, f32[16]{0:T(128)S(1)}, u32[]{:S(2)}, u32[]{:S(2)}) %collective-permute-start) | collective-permute-done | bytes 96 | tf_op jit(solution)/shard_map/ppermute | solution.py:16
  65.3 6.0 collective-permute-start.1
  71.3 0.7 collective-permute-done.1
  72.3 47.0 %collective-permute-start.7 = (bf16[16,16384]{1,0:T(8,128)(2,1)S(1)}, bf16[16,16384]{1,0:T(8,128)(2,1)S(1)}, u32[]{:S(2)}, u32[]{:S(2)}) collective-permute-start(bf16[16,16384]{1,0:T(8,128)(2,1)S(1)} %fusion.31), channel_id=1, source_target_pairs={{0,16},{8,24},{16,32},{24,40},{32,48},{40,56},{48,64},{56,72},{64,... | collective-permute-start | bytes 1572872 | tf_op jit(solution)/shard_map/ppermute | solution.py:17
  119.4 6.0 collective-permute-done.7
  125.7 6.6 %collective-permute-start.8 = (bf16[16,16384]{1,0:T(8,128)(2,1)S(1)}, bf16[16,16384]{1,0:T(8,128)(2,1)S(1)}, u32[]{:S(2)}, u32[]{:S(2)}) collective-permute-start(bf16[16,16384]{1,0:T(8,128)(2,1)S(1)} %fusion.39), channel_id=1, source_target_pairs={{0,32},{8,40},{16,48},{24,56},{32,64},{40,72},{48,80},{56,88},{64,... | collective-permute-start | bytes 1572872 | tf_op jit(solution)/shard_map/ppermute | solution.py:17
  132.3 1.3 collective-permute-start.2
  133.6 12.1 %collective-permute-done.2 = f32[16]{0:T(128)S(1)} collective-permute-done((f32[16]{0:T(128)S(1)}, f32[16]{0:T(128)S(1)}, u32[]{:S(2)}, u32[]{:S(2)}) %collective-permute-start.2) | collective-permute-done | bytes 96 | tf_op jit(solution)/shard_map/ppermute | solution.py:16
  146.2 17.2 %collective-permute-start.9 = (bf16[16,16384]{1,0:T(8,128)(2,1)S(1)}, bf16[16,16384]{1,0:T(8,128)(2,1)S(1)}, u32[]{:S(2)}, u32[]{:S(2)}) collective-permute-start(bf16[16,16384]{1,0:T(8,128)(2,1)S(1)} %fusion.32), channel_id=1, source_target_pairs={{0,64},{8,72},{16,80},{24,88},{32,96},{40,104},{48,112},{56,120},{... | collective-permute-start | bytes 1572872 | tf_op jit(solution)/shard_map/ppermute | solution.py:17
  163.4 1.4 collective-permute-start.3
  164.8 0.7 collective-permute-done.3
  165.5 3.9 collective-permute-done.9
  169.4 1.3 fusion.38
  170.7 17.4 %collective-permute-start.10 = (bf16[16,16384]{1,0:T(8,128)(2,1)}, bf16[16,16384]{1,0:T(8,128)(2,1)}, u32[]{:S(2)}, u32[]{:S(2)}) collective-permute-start(bf16[16,16384]{1,0:T(8,128)(2,1)} %fusion.38), channel_id=1, source_target_pairs={{0,128},{8,136},{16,144},{24,152},{32,160},{40,168},{48,176},{56,1... | collective-permute-start | bytes 1572872 | tf_op jit(solution)/shard_map/ppermute | solution.py:17
  188.1 4.1 reshape.189
  192.3 4.6 copy.44
  197.0 1.1 fusion.44
  198.1 1.8 collective-permute-start.4
  199.8 2.2 convert_element_type.98
  202.0 1.8 multiply_add_fusion
  203.9 0.8 mul.195
  205.3 5.3 fusion.21
  210.7 3.1 multiply_reduce_fusion
  213.8 1.6 copy.45
  215.9 11.3 %all-gather.7.cloned.1.call-done = bf16[1024,4096]{1,0:T(8,128)(2,1)} async-done(((bf16[1024,128]{1,0:T(8,128)(2,1)}), bf16[1024,4096]{1,0:T(8,128)(2,1)}) %all-gather.7.cloned.1.call-update) | async-done | bytes 8388624 | tf_op jit(solution)/shard_map/all_gather | solution.py:119
  227.2 9.7 %fusion.4 = bf16[512,4096]{1,0:T(8,128)(2,1)} fusion(bf16[512,1024]{0,1:T(8,128)(2,1)S(1)} %multiply_convert_fusion.4, bf16[1024,4096]{1,0:T(8,128)(2,1)} %all-gather.7.cloned.1.call-done, f32[64,4096]{1,0:T(8,128)S(1)} %copy-done.7, pred[512]{0:T(512)(128)(4,1)S(1)} %broadcast_in_dim.63), kind=kOutput, calls=%fused_computation.7 | convolution fusion | flops 4301258752 | bytes 14680576 | tf_op jit(solution)/shard_map/dot_general | solution.py:117
  237.0 0.7 copy-done.10
  239.0 326.3 %all-gather.9.cloned.1.call-done = bf16[4096,4096]{1,0:T(8,128)(2,1)} async-done(((bf16[512,4096]{1,0:T(8,128)(2,1)}), bf16[4096,4096]{1,0:T(8,128)(2,1)}) %all-gather.9.cloned.1.call-update) | async-done | bytes 33554448 | tf_op jit(solution)/shard_map/all_gather | solution.py:123
  565.3 14.0 %reduce_sum.50 = bf16[512,4096]{1,0:T(8,128)(2,1)} reduce(bf16[8,512,4096]{2,1,0:T(8,128)(2,1)} %bitcast.68, bf16[]{:T(256)} %constant.10.clone.1), dimensions={0}, to_apply=%region_5.6 | reduce | flops 14680064 | bytes 37748736 | tf_op jit(solution)/shard_map/reduce_sum | solution.py:123
  579.4 4.6 fusion.45
  584.0 1.9 fusion
  585.9 0.8 constant_dynamic-slice_fusion
  586.8 8.2 %fusion.26 = bf16[512,1024]{1,0:T(8,128)(2,1)} fusion(bf16[4096,1024]{1,0:T(8,128)(2,1)} %all-gather.5.cloned.1.call-done, bf16[512,4096]{1,0:T(8,128)(2,1)S(1)} %get-tuple-element.11, f32[4096]{0:T(1024)S(1)} %copy-done.13, f32[512]{0:T(512)S(1)} %add_rsqrt_fusion), kind=kOutput, calls=%fused_computation.34 | convolution fusion | flops 4303880192 | bytes 13649920 | tf_op jit(solution)/shard_map/dot_general | solution.py:134
  (69 shorter events, 5.7 us)
Async XLA Ops:
  7.2 189.8 %copy-start = (bf16[512,1,256]{2,0,1:T(8,128)(2,1)S(1)}, bf16[512,1,256]{2,0,1:T(8,128)(2,1)}, u32[]{:S(2)}) copy-start(bf16[512,1,256]{2,0,1:T(8,128)(2,1)} %param.15) | copy-start | bytes 786436
  7.2 208.8 %all-gather.5.cloned.1.call-start = ((), (), s32[]{:S(2)}) async-start(), calls=%async_computation | async-start | bytes 8650752 | tf_op jit(solution)/shard_map/all_gather | solution.py:108
  7.9 219.3 %all-gather.7.cloned.1.call-start = ((), (), s32[]{:S(2)}) async-start(), calls=%async_computation.1 | async-start | bytes 8650752 | tf_op jit(solution)/shard_map/all_gather | solution.py:119
  14.7 5.6 copy-start.5
  26.4 21.5 %collective-permute-start.5 = (bf16[16,16384]{1,0:T(8,128)(2,1)S(1)}, bf16[16,16384]{1,0:T(8,128)(2,1)S(1)}, u32[]{:S(2)}, u32[]{:S(2)}) collective-permute-start(bf16[16,16384]{1,0:T(8,128)(2,1)S(1)} %add_convert_fusion), channel_id=1, source_target_pairs={{0,8},{8,16},{16,24},{24,32},{32,40},{40,48},{48,56},{56,64},{64,7... | collective-permute-start | bytes 1572872 | tf_op jit(solution)/shard_map/ppermute | solution.py:17
  47.9 24.1 %collective-permute-start.6 = (bf16[16,16384]{1,0:T(8,128)(2,1)S(1)}, bf16[16,16384]{1,0:T(8,128)(2,1)S(1)}, u32[]{:S(2)}, u32[]{:S(2)}) collective-permute-start(bf16[16,16384]{1,0:T(8,128)(2,1)S(1)} %collective-permute-done.5), channel_id=1, source_target_pairs={{0,8},{8,16},{16,24},{24,32},{32,40},{40,48},{48,56},{56,64},{64,7... | collective-permute-start | bytes 1572872 | tf_op jit(solution)/shard_map/ppermute | solution.py:17
  53.2 12.1 %collective-permute-start = (f32[16]{0:T(128)S(1)}, f32[16]{0:T(128)S(1)}, u32[]{:S(2)}, u32[]{:S(2)}) collective-permute-start(f32[16]{0:T(128)S(1)} %get-tuple-element.6), channel_id=1, source_target_pairs={{0,8},{8,16},{16,24},{24,32},{32,40},{40,48},{48,56},{56,64},{64,7... | collective-permute-start | bytes 200 | tf_op jit(solution)/shard_map/ppermute | solution.py:16
  65.3 6.7 %collective-permute-start.1 = (f32[16]{0:T(128)S(1)}, f32[16]{0:T(128)S(1)}, u32[]{:S(2)}, u32[]{:S(2)}) collective-permute-start(f32[16]{0:T(128)S(1)} %collective-permute-done), channel_id=1, source_target_pairs={{0,8},{8,16},{16,24},{24,32},{32,40},{40,48},{48,56},{56,64},{64,7... | collective-permute-start | bytes 200 | tf_op jit(solution)/shard_map/ppermute | solution.py:16
  72.3 53.1 %collective-permute-start.7 = (bf16[16,16384]{1,0:T(8,128)(2,1)S(1)}, bf16[16,16384]{1,0:T(8,128)(2,1)S(1)}, u32[]{:S(2)}, u32[]{:S(2)}) collective-permute-start(bf16[16,16384]{1,0:T(8,128)(2,1)S(1)} %fusion.31), channel_id=1, source_target_pairs={{0,16},{8,24},{16,32},{24,40},{32,48},{40,56},{48,64},{56,72},{64,... | collective-permute-start | bytes 1572872 | tf_op jit(solution)/shard_map/ppermute | solution.py:17
  119.3 446.0 %all-gather.9.cloned.1.call-start = ((), (), s32[]{:S(2)}) async-start(), calls=%async_computation.2 | async-start | bytes 37748736 | tf_op jit(solution)/shard_map/all_gather | solution.py:123
  125.7 20.0 %collective-permute-start.8 = (bf16[16,16384]{1,0:T(8,128)(2,1)S(1)}, bf16[16,16384]{1,0:T(8,128)(2,1)S(1)}, u32[]{:S(2)}, u32[]{:S(2)}) collective-permute-start(bf16[16,16384]{1,0:T(8,128)(2,1)S(1)} %fusion.39), channel_id=1, source_target_pairs={{0,32},{8,40},{16,48},{24,56},{32,64},{40,72},{48,80},{56,88},{64,... | collective-permute-start | bytes 1572872 | tf_op jit(solution)/shard_map/ppermute | solution.py:17
  132.3 13.4 %collective-permute-start.2 = (f32[16]{0:T(128)S(1)}, f32[16]{0:T(128)S(1)}, u32[]{:S(2)}, u32[]{:S(2)}) collective-permute-start(f32[16]{0:T(128)S(1)} %get-tuple-element.17), channel_id=1, source_target_pairs={{0,16},{8,24},{16,32},{24,40},{32,48},{40,56},{48,64},{56,72},{64,... | collective-permute-start | bytes 200 | tf_op jit(solution)/shard_map/ppermute | solution.py:16
  146.2 23.3 %collective-permute-start.9 = (bf16[16,16384]{1,0:T(8,128)(2,1)S(1)}, bf16[16,16384]{1,0:T(8,128)(2,1)S(1)}, u32[]{:S(2)}, u32[]{:S(2)}) collective-permute-start(bf16[16,16384]{1,0:T(8,128)(2,1)S(1)} %fusion.32), channel_id=1, source_target_pairs={{0,64},{8,72},{16,80},{24,88},{32,96},{40,104},{48,112},{56,120},{... | collective-permute-start | bytes 1572872 | tf_op jit(solution)/shard_map/ppermute | solution.py:17
  163.4 2.1 collective-permute-start.3
  169.4 22.8 %copy-start.4 = (bf16[16,16384]{1,0:T(8,128)(2,1)}, bf16[16,16384]{1,0:T(8,128)(2,1)S(1)}, u32[]{:S(2)}) copy-start(bf16[16,16384]{1,0:T(8,128)(2,1)S(1)} %collective-permute-done.9) | copy-start | bytes 1572868
  170.7 31.3 %collective-permute-start.10 = (bf16[16,16384]{1,0:T(8,128)(2,1)}, bf16[16,16384]{1,0:T(8,128)(2,1)}, u32[]{:S(2)}, u32[]{:S(2)}) collective-permute-start(bf16[16,16384]{1,0:T(8,128)(2,1)} %fusion.38), channel_id=1, source_target_pairs={{0,128},{8,136},{16,144},{24,152},{32,160},{40,168},{48,176},{56,1... | collective-permute-start | bytes 1572872 | tf_op jit(solution)/shard_map/ppermute | solution.py:17
  192.3 4.8 copy-start.8
  198.1 3.9 collective-permute-start.4
  204.7 6.0 copy-start.11
  204.7 6.0 copy-start.14
  205.3 5.4 copy-start.3
  205.3 5.4 copy-start.6
  205.3 5.4 copy-start.9
  213.8 1.9 copy-start.12
  215.4 11.8 %copy-start.7 = (f32[64,4096]{1,0:T(8,128)S(1)}, f32[64,4096]{1,0:T(8,128)}, u32[]{:S(2)}) copy-start(f32[64,4096]{1,0:T(8,128)} %convert_element_type.98) | copy-start | bytes 3145732
  237.0 0.7 copy-start.10
  579.4 4.6 copy-start.2
  584.0 2.8 copy-start.13
  586.8 8.2 %copy-start.1 = (bf16[512,1,256]{2,0,1:T(8,128)(2,1)S(1)}, bf16[512,1,256]{2,0,1:T(8,128)(2,1)}, u32[]{:S(2)}) copy-start(bf16[512,1,256]{2,0,1:T(8,128)(2,1)} %param.15) | copy-start | bytes 786436
Sparse Core Ops, SparseCore 0:
  10.6 109.2 all-gather.4
  122.3 104.8 all-gather.6
  237.1 328.1 all-gather.8
